TPU v7x, 256 devices: a whole 4x4x8 slice. The times are simulated.
256 devices in a mesh: axial: 16 (over x_lo, y, core), azim: 16 (over z, x_hi).
Axes of the slice: x: 4 (x_hi: 2, x_lo: 2; x = x_hi * 2 + x_lo), y: 4, z: 8, core: 2. Of those that a mesh axis runs over, the one named last changes fastest.
Arguments:
- coil_density: float32 [512, 256, 128], P('azim', 'axial'), may hold values from -6 to 6
- coil_mask: int32 [512, 256, 128], P('azim', 'axial'), may hold values 0 or 1
- drive: float32 [2], replicated, may hold values from 0.5 to 2
- potential: float32 [512, 256, 128], P('azim', 'axial'), may hold values from -6 to 6
- tile_weight: float32 [512, 64, 64], P('azim'), may hold values from -0.75 to 0.75
- relay_owner: int32 [2, 512, 16], P(None, 'azim', 'axial'), may hold values from 0 to 2
- relay_slot: int32 [2, 512, 16], P(None, 'azim', 'axial'), may hold values from 0 to 31, as said below
- velocity: float32 [512, 256, 128], P('azim', 'axial'), may hold values from -3 to 3
- strain: float32 [512, 256, 128], P('azim', 'axial'), may hold values from -3 to 3
- plastic: float32 [512, 256, 128], P('azim', 'axial'), may hold values from -0.6 to 0.6
Outputs:
- field_out: float32 [512, 256, 128], P('azim', 'axial')
- velocity_out: float32 [512, 256, 128], P('azim', 'axial')
- strain_out: float32 [512, 256, 128], P('azim', 'axial')
- plastic_out: float32 [512, 256, 128], P('azim', 'axial')
Inputs may be any that keep to these rules, and one draw needn't show every extreme that they name: `relay_slot`: for each step and axial block, the values over the 32 azimuthal cells of one sector are a permutation of 0 to 31.
All inputs are finite; a program needn't handle non-finite values. No bound on the sum of `coil_mask` on one device may be relied on, other than what follows from the above.
Results may differ from a plain program's by a relative error of at most 0.00011.
Values sent between devices are 32-bit elements; how exact they have to be, the bound alone decides.
No kernel may reach another device: no remote copies, remote signals or barrier semaphores. Data moves between devices by JAX's collectives and lax.ppermute only.
A program may use at most 64 MiB of HBM per device.

v0:
```python
import math
import jax
import jax.numpy as jnp
from jax import lax
from jax.sharding import PartitionSpec as P

STEPS = 2
SWEEPS = 3
HIGH = lax.Precision.HIGHEST
KAPPA = 2.0
AIR_TERM = 0.05
R_CORE = 16.0
MU_COIL = 1.0
FORCE_K = 1.0
E_MOD = 1.0
YIELD_ZERO = 0.5
HARDEN = 0.3
TIME_STEP = 0.5
STIFFNESS = 0.5
DAMPING = 0.9


def with_halo(block, sides, width):
    for axis, dim in sides:
        count = lax.axis_size(axis)
        forward = [(i, i + 1) for i in range(count - 1)]
        backward = [(target, source) for source, target in forward]
        low = lax.ppermute(
            lax.slice_in_dim(block, block.shape[dim] - width, None, axis=dim), axis, forward
        )
        high = lax.ppermute(lax.slice_in_dim(block, 0, width, axis=dim), axis, backward)
        block = jnp.concatenate([low, block, high], axis=dim)
    return block


def shifted(array, axis, by):
    devices = lax.axis_size(axis)
    pairs = [(i, i + by) for i in range(devices) if 0 <= i + by < devices]
    return lax.ppermute(array, axis, pairs)


def harmonic_table(azimuth, harmonic, count_all):
    half_count = count_all // 2
    orders = jnp.where(harmonic <= half_count, harmonic, harmonic - half_count)
    phases = azimuth[:, None] * orders[None, :] % count_all
    angles = phases.astype(jnp.float32) * (2.0 * math.pi / count_all)
    return jnp.where(harmonic[None, :] <= half_count, jnp.cos(angles), jnp.sin(angles))


def harmonic_weight(harmonic, count_all):
    half_count = count_all // 2
    edge_mode = (harmonic == 0) | (harmonic == half_count)
    return jnp.where(edge_mode, 1.0 / count_all, 2.0 / count_all).astype(jnp.float32)


def harmonic_order(harmonic, count_all):
    half_count = count_all // 2
    return jnp.where(harmonic <= half_count, harmonic, harmonic - half_count).astype(jnp.float32)


def radial_profiles(radial_count, band_start, band_width):
    cell_index = jnp.arange(radial_count, dtype=jnp.int32)
    radius = R_CORE + cell_index.astype(jnp.float32)
    inside = (cell_index >= band_start) & (cell_index < band_start + band_width)
    conduct = jnp.where(inside, KAPPA, AIR_TERM).astype(jnp.float32)
    coil_zone = (cell_index < band_start).astype(jnp.float32)
    return (radius, conduct, coil_zone)


def radial_sum(iterate):
    radial_pad = jnp.pad(iterate, ((0, 0), (0, 0), (1, 1)))
    return radial_pad[:, :, 2:] + radial_pad[:, :, :-2]


def lorentz(padded, previous, conduct, radius, band_start, band_width):
    current_field = padded[:, 1:-1]
    axial_slope = (padded[:, 2:] - padded[:, :-2]) * 0.5
    radial_pad = jnp.pad(current_field, ((0, 0), (0, 0), (1, 1)))
    radial_slope = (radial_pad[:, :, 2:] - radial_pad[:, :, :-2]) * 0.5
    b_axial = radial_slope + current_field / radius
    eddy_current = -conduct * (current_field - previous)
    force_radial = FORCE_K * eddy_current * b_axial
    force_axial = FORCE_K * eddy_current * axial_slope
    return jnp.concatenate(
        [
            force_radial[..., band_start : band_start + band_width],
            force_axial[..., band_start : band_start + band_width],
        ],
        axis=-1,
    )


def plastic_update(load, velocity, strain, plastic):
    trial_stress = E_MOD * (strain - plastic)
    excess = jnp.abs(trial_stress) - YIELD_ZERO
    increment = (
        trial_stress
        * jnp.maximum(excess, 0.0)
        / ((E_MOD + HARDEN) * jnp.maximum(jnp.abs(trial_stress), YIELD_ZERO))
    )
    plastic = plastic + increment
    stress = E_MOD * (strain - plastic)
    velocity = DAMPING * velocity + TIME_STEP * (load - STIFFNESS * stress)
    strain = strain + TIME_STEP * velocity
    return (velocity, strain, plastic)


def transform(parts, table_rows, all_index):
    flat_shape = parts.shape
    columns_all = parts.reshape(flat_shape[0], -1)
    spread = lax.all_to_all(columns_all, "azim", split_axis=1, concat_axis=0, tiled=True)
    full_table = table_rows(all_index, all_index)
    mixed = jnp.dot(full_table.T, spread, precision=HIGH, preferred_element_type=jnp.float32)
    joined = lax.all_to_all(mixed, "azim", split_axis=0, concat_axis=1, tiled=True)
    return joined.reshape(flat_shape)


def shards(
    coil_density,
    coil_mask,
    drive,
    potential,
    tile_weight,
    relay_owner,
    relay_slot,
    velocity,
    strain,
    plastic,
):
    local_count = potential.shape[0]
    axial_cells = potential.shape[1]
    radial_cells = potential.shape[2]
    band_width = tile_weight.shape[1]
    azim_total = local_count * lax.axis_size("azim")
    own_index = lax.axis_index("azim") * local_count + jnp.arange(local_count, dtype=jnp.int32)
    all_index = jnp.arange(azim_total, dtype=jnp.int32)
    band_start = radial_cells // 4
    radius, conduct, coil_zone = radial_profiles(radial_cells, band_start, band_width)
    orders = harmonic_order(own_index, azim_total)
    diagonal_term = (
        4.0 + conduct[None, None, :] + (orders[:, None, None] / radius[None, None, :]) ** 2
    )

    def forward_rows(rows_in, rows_out):
        return harmonic_table(rows_in, rows_out, azim_total)

    def inverse_rows(rows_in, rows_out):
        return (
            harmonic_table(rows_out, rows_in, azim_total).T
            * harmonic_weight(rows_in, azim_total)[:, None]
        )

    slot_range = jnp.arange(local_count, dtype=jnp.int32)
    field = potential
    for step_index in range(STEPS):
        source = drive[step_index] * coil_density * coil_mask.astype(jnp.float32) * coil_zone
        stacked = jnp.stack([source, field], axis=1)
        modes = transform(stacked, forward_rows, all_index)
        right_side = MU_COIL * modes[:, 0] + conduct * modes[:, 1]
        iterate = modes[:, 1]
        for sweep_index in range(SWEEPS):
            axial_pad = with_halo(iterate, (("axial", 1),), 1)
            nearby = axial_pad[:, 2:] + axial_pad[:, :-2] + radial_sum(iterate)
            iterate = (right_side + nearby) / diagonal_term
        new_field = transform(iterate[:, None], inverse_rows, all_index)[:, 0]
        padded = with_halo(new_field, (("axial", 1),), 1)
        tiles = lorentz(padded, field, conduct, radius, band_start, band_width)
        slot_table = (relay_slot[step_index, :, 0][:, None] == slot_range[None, :]).astype(
            jnp.float32
        )
        owner_now = relay_owner[step_index, :, 0]

        def place(target):
            chosen = (owner_now == target).astype(jnp.float32)
            return jnp.einsum(
                "jcw,jp->pcw", tiles * chosen[:, None, None], slot_table, precision=HIGH
            )

        from_below = shifted(place(2), "axial", 1)
        from_above = shifted(place(0), "axial", -1)
        received = (place(1) + from_below + from_above).reshape(
            local_count, axial_cells, 2, band_width
        )
        load = jnp.einsum("aqr,azcr->azcq", tile_weight, received, precision=HIGH).reshape(
            local_count, axial_cells, 2 * band_width
        )
        velocity, strain, plastic = plastic_update(load, velocity, strain, plastic)
        field = new_field
    return (field, velocity, strain, plastic)


def solution(mesh):
    placed = (
        P("azim", "axial", None),
        P("azim", "axial", None),
        P(),
        P("azim", "axial", None),
        P("azim", None, None),
        P(None, "azim", "axial"),
        P(None, "azim", "axial"),
        P("azim", "axial", None),
        P("azim", "axial", None),
        P("azim", "axial", None),
    )
    return jax.shard_map(
        shards,
        mesh=mesh,
        in_specs=placed,
        out_specs=(
            P("azim", "axial", None),
            P("azim", "axial", None),
            P("azim", "axial", None),
            P("azim", "axial", None),
        ),
        check_vma=False,
    )
```

profile of v0, /device:TPU:25, one launch (start us, length us, event | category | flops | bytes accessed | tf_op | source)
XLA Modules:
  0.0 291.4 jit_solution(16157686865284336224)
XLA Ops:
  0.7 0.7 copy-done.5
  1.4 0.6 fusion.134
  2.0 2.6 multiply_bitcast_fusion.1
  5.1 1.1 copy.68
  6.2 10.7 %all-to-all-start = ((f32[32,16,256]{2,0,1:T(8,128)}), f32[32,16,256]{2,0,1:T(8,128)S(1)}, u32[]{:S(2)}, u32[]{:S(2)}) async-start(f32[32,16,256]{2,0,1:T(8,128)} %copy.68), calls=%async_computation | async-start | bytes 1048576 | tf_op jit(solution)/shard_map/all_to_all | solution.py:111
  17.0 17.2 %all-to-all-done = f32[32,16,256]{2,0,1:T(8,128)S(1)} async-done(((f32[32,16,256]{2,0,1:T(8,128)}), f32[32,16,256]{2,0,1:T(8,128)S(1)}, u32[]{:S(2)}, u32[]{:S(2)}) %all-to-all-start) | async-done | bytes 524320 | tf_op jit(solution)/shard_map/all_to_all | solution.py:111
  34.2 8.6 %fusion.14 = f32[16,32,256]{2,1,0:T(8,128)} fusion(f32[512,256,1]{1,0,2:T(8,128)S(1)} %bitcast.139, s32[16,32]{1,0:T(8,128)S(1)} %add_select_fusion.2, pred[16,32]{1,0:T(8,128)(4,1)S(1)} %fusion.99), kind=kOutput, calls=%fused_computation.24 | convolution fusion | flops 809238528 | bytes 1051136 | tf_op jit(solution)/shard_map/dot_general | solution.py:113
  42.8 4.7 %all-to-all-start.1 = ((f32[16,32,256]{2,1,0:T(8,128)}), f32[16,32,256]{2,1,0:T(8,128)S(1)}, u32[]{:S(2)}, u32[]{:S(2)}) async-start(f32[16,32,256]{2,1,0:T(8,128)} %fusion.14), calls=%async_computation.1 | async-start | bytes 1048576 | tf_op jit(solution)/shard_map/all_to_all | solution.py:114
  47.6 17.2 %all-to-all-done.1 = f32[16,32,256]{2,1,0:T(8,128)S(1)} async-done(((f32[16,32,256]{2,1,0:T(8,128)}), f32[16,32,256]{2,1,0:T(8,128)S(1)}, u32[]{:S(2)}, u32[]{:S(2)}) %all-to-all-start.1) | async-done | bytes 524320 | tf_op jit(solution)/shard_map/all_to_all | solution.py:114
  65.3 4.3 %collective-permute-start = (f32[32,1,128]{2,1,0:T(1,128)S(1)}, f32[32,1,128]{2,1,0:T(1,128)S(1)}, u32[]{:S(2)}, u32[]{:S(2)}) collective-permute-start(f32[32,1,128]{2,1,0:T(1,128)S(1)} %get-tuple-element.45), channel_id=1, source_target_pairs={{16,0},{32,16},{48,32},{64,48},{80,64},{96,80},{112,96},{128,112},... | collective-permute-start | bytes 49160 | tf_op jit(solution)/shard_map/ppermute | solution.py:31
  69.6 3.4 %collective-permute-start.1 = (f32[32,1,128]{2,1,0:T(1,128)S(1)}, f32[32,1,128]{2,1,0:T(1,128)S(1)}, u32[]{:S(2)}, u32[]{:S(2)}) collective-permute-start(f32[32,1,128]{2,1,0:T(1,128)S(1)} %get-tuple-element.46), channel_id=1, source_target_pairs={{0,16},{16,32},{32,48},{48,64},{64,80},{80,96},{96,112},{112,128},... | collective-permute-start | bytes 49160 | tf_op jit(solution)/shard_map/ppermute | solution.py:28
  73.0 0.8 collective-permute-done.1
  74.1 2.7 collective-permute-start.2
  76.8 5.5 %collective-permute-start.3 = (f32[32,1,128]{2,1,0:T(1,128)S(1)}, f32[32,1,128]{2,1,0:T(1,128)S(1)}, u32[]{:S(2)}, u32[]{:S(2)}) collective-permute-start(f32[32,1,128]{2,1,0:T(1,128)S(1)} %get-tuple-element.44), channel_id=1, source_target_pairs={{0,16},{16,32},{32,48},{48,64},{64,80},{80,96},{96,112},{112,128},... | collective-permute-start | bytes 49160 | tf_op jit(solution)/shard_map/ppermute | solution.py:28
  82.3 0.8 collective-permute-done.3
  83.4 1.9 collective-permute-start.4
  85.4 6.3 %collective-permute-start.5 = (f32[32,1,128]{2,1,0:T(1,128)S(1)}, f32[32,1,128]{2,1,0:T(1,128)S(1)}, u32[]{:S(2)}, u32[]{:S(2)}) collective-permute-start(f32[32,1,128]{2,1,0:T(1,128)S(1)} %get-tuple-element.42), channel_id=1, source_target_pairs={{0,16},{16,32},{32,48},{48,64},{64,80},{80,96},{96,112},{112,128},... | collective-permute-start | bytes 49160 | tf_op jit(solution)/shard_map/ppermute | solution.py:28
  91.7 0.8 collective-permute-done.5
  92.7 0.8 copy.71
  93.5 4.2 %all-to-all-start.2 = ((f32[32,16,128]{2,0,1:T(8,128)}), f32[32,16,128]{2,0,1:T(8,128)S(1)}, u32[]{:S(2)}, u32[]{:S(2)}) async-start(f32[32,16,128]{2,0,1:T(8,128)} %copy.71), calls=%async_computation.2 | async-start | bytes 524288 | tf_op jit(solution)/shard_map/all_to_all | solution.py:111
  97.7 11.1 %all-to-all-done.2 = f32[32,16,128]{2,0,1:T(8,128)S(1)} async-done(((f32[32,16,128]{2,0,1:T(8,128)}), f32[32,16,128]{2,0,1:T(8,128)S(1)}, u32[]{:S(2)}, u32[]{:S(2)}) %all-to-all-start.2) | async-done | bytes 262176 | tf_op jit(solution)/shard_map/all_to_all | solution.py:111
  108.8 5.1 %fusion.22 = f32[16,32,128]{2,1,0:T(8,128)S(1)} fusion(f32[512,128,1]{1,0,2:T(8,128)S(1)} %bitcast.142, f32[512]{0:T(512)S(1)} %fusion.101, s32[512]{0:T(512)S(1)} %add_select_fusion.3, s32[16,32]{1,0:T(8,128)S(1)} %multiply_add_fusion.3, pred[512]{0:T(512)(128)(4,1)S(1)} %iota_compare_fusion.4), kind=kOutput, calls=%fused_computation.52 | convolution fusion | flops 406847488 | bytes 530944 | tf_op jit(solution)/shard_map/dot_general | solution.py:113
  114.0 14.8 %all_to_all.122 = f32[16,32,128]{2,1,0:T(8,128)S(1)} all-to-all(f32[16,32,128]{2,1,0:T(8,128)S(1)} %fusion.22), channel_id=1, replica_groups=mesh['axial'=16,'azim'=16] {'azim'}, dimensions={0} | all-to-all | bytes 524288 | tf_op jit(solution)/shard_map/all_to_all | solution.py:114
  129.6 21.7 %all_to_all.123 = f32[32,16,256]{2,0,1:T(8,128)S(1)} all-to-all(f32[32,16,256]{2,0,1:T(8,128)S(1)} %copy.73), channel_id=1, replica_groups=mesh['axial'=16,'azim'=16] {'azim'}, dimensions={1} | all-to-all | bytes 1048576 | tf_op jit(solution)/shard_map/all_to_all | solution.py:111
  151.3 8.0 %fusion.12 = f32[16,32,256]{2,1,0:T(8,128)S(1)} fusion(f32[512,256,1]{1,0,2:T(8,128)S(1)} %bitcast.140, s32[16,32]{1,0:T(8,128)S(1)} %add_select_fusion.2, pred[16,32]{1,0:T(8,128)(4,1)S(1)} %fusion.99), kind=kOutput, calls=%fused_computation.22 | convolution fusion | flops 809238528 | bytes 1051136 | tf_op jit(solution)/shard_map/dot_general | solution.py:113
  159.3 20.4 %all_to_all.124 = f32[16,32,256]{2,1,0:T(8,128)S(1)} all-to-all(f32[16,32,256]{2,1,0:T(8,128)S(1)} %fusion.12), channel_id=1, replica_groups=mesh['axial'=16,'azim'=16] {'azim'}, dimensions={0} | all-to-all | bytes 1048576 | tf_op jit(solution)/shard_map/all_to_all | solution.py:114
  180.1 4.5 %collective-permute-start.6 = (f32[32,1,128]{2,1,0:T(1,128)S(1)}, f32[32,1,128]{2,1,0:T(1,128)S(1)}, u32[]{:S(2)}, u32[]{:S(2)}) collective-permute-start(f32[32,1,128]{2,1,0:T(1,128)S(1)} %get-tuple-element.39), channel_id=1, source_target_pairs={{16,0},{32,16},{48,32},{64,48},{80,64},{96,80},{112,96},{128,112},... | collective-permute-start | bytes 49160 | tf_op jit(solution)/shard_map/ppermute | solution.py:31
  184.6 3.2 %collective-permute-start.7 = (f32[32,1,128]{2,1,0:T(1,128)S(1)}, f32[32,1,128]{2,1,0:T(1,128)S(1)}, u32[]{:S(2)}, u32[]{:S(2)}) collective-permute-start(f32[32,1,128]{2,1,0:T(1,128)S(1)} %get-tuple-element.40), channel_id=1, source_target_pairs={{0,16},{16,32},{32,48},{48,64},{64,80},{80,96},{96,112},{112,128},... | collective-permute-start | bytes 49160 | tf_op jit(solution)/shard_map/ppermute | solution.py:28
  187.8 0.8 collective-permute-done.7
  188.9 3.0 %collective-permute-start.8 = (f32[32,1,128]{2,1,0:T(1,128)S(1)}, f32[32,1,128]{2,1,0:T(1,128)S(1)}, u32[]{:S(2)}, u32[]{:S(2)}) collective-permute-start(f32[32,1,128]{2,1,0:T(1,128)S(1)} %get-tuple-element.37), channel_id=1, source_target_pairs={{16,0},{32,16},{48,32},{64,48},{80,64},{96,80},{112,96},{128,112},... | collective-permute-start | bytes 49160 | tf_op jit(solution)/shard_map/ppermute | solution.py:31
  191.8 5.3 %collective-permute-start.9 = (f32[32,1,128]{2,1,0:T(1,128)S(1)}, f32[32,1,128]{2,1,0:T(1,128)S(1)}, u32[]{:S(2)}, u32[]{:S(2)}) collective-permute-start(f32[32,1,128]{2,1,0:T(1,128)S(1)} %get-tuple-element.38), channel_id=1, source_target_pairs={{0,16},{16,32},{32,48},{48,64},{64,80},{80,96},{96,112},{112,128},... | collective-permute-start | bytes 49160 | tf_op jit(solution)/shard_map/ppermute | solution.py:28
  197.1 0.8 collective-permute-done.9
  198.2 1.9 collective-permute-start.10
  200.1 6.3 %collective-permute-start.11 = (f32[32,1,128]{2,1,0:T(1,128)S(1)}, f32[32,1,128]{2,1,0:T(1,128)S(1)}, u32[]{:S(2)}, u32[]{:S(2)}) collective-permute-start(f32[32,1,128]{2,1,0:T(1,128)S(1)} %get-tuple-element.36), channel_id=1, source_target_pairs={{0,16},{16,32},{32,48},{48,64},{64,80},{80,96},{96,112},{112,128},... | collective-permute-start | bytes 49160 | tf_op jit(solution)/shard_map/ppermute | solution.py:28
  206.5 0.8 collective-permute-done.11
  207.5 0.8 copy.77
  208.3 4.2 %all-to-all-start.6 = ((f32[32,16,128]{2,0,1:T(8,128)}), f32[32,16,128]{2,0,1:T(8,128)S(1)}, u32[]{:S(2)}, u32[]{:S(2)}) async-start(f32[32,16,128]{2,0,1:T(8,128)} %copy.77), calls=%async_computation.6 | async-start | bytes 524288 | tf_op jit(solution)/shard_map/all_to_all | solution.py:111
  212.6 11.1 %all-to-all-done.6 = f32[32,16,128]{2,0,1:T(8,128)S(1)} async-done(((f32[32,16,128]{2,0,1:T(8,128)}), f32[32,16,128]{2,0,1:T(8,128)S(1)}, u32[]{:S(2)}, u32[]{:S(2)}) %all-to-all-start.6) | async-done | bytes 262176 | tf_op jit(solution)/shard_map/all_to_all | solution.py:111
  223.7 6.8 %fusion.21 = f32[16,32,128]{2,1,0:T(8,128)} fusion(f32[512,128,1]{1,0,2:T(8,128)S(1)} %bitcast.141, f32[512]{0:T(512)S(1)} %fusion.101, s32[512]{0:T(512)S(1)} %add_select_fusion.3, s32[16,32]{1,0:T(8,128)S(1)} %multiply_add_fusion.3, pred[512]{0:T(512)(128)(4,1)S(1)} %iota_compare_fusion.4), kind=kOutput, calls=%fused_computation.51 | convolution fusion | flops 406847488 | bytes 530944 | tf_op jit(solution)/shard_map/dot_general | solution.py:113
  230.5 3.7 %all-to-all-start.7 = ((f32[16,32,128]{2,1,0:T(8,128)}), f32[16,32,128]{2,1,0:T(8,128)S(1)}, u32[]{:S(2)}, u32[]{:S(2)}) async-start(f32[16,32,128]{2,1,0:T(8,128)} %fusion.21), calls=%async_computation.7 | async-start | bytes 524288 | tf_op jit(solution)/shard_map/all_to_all | solution.py:114
  234.2 1.9 collective-permute-start.12
  236.2 7.9 %collective-permute-start.13 = (f32[32,1,128]{2,0,1:T(8,128)S(1)}, f32[32,1,128]{2,0,1:T(8,128)S(1)}, u32[]{:S(2)}, u32[]{:S(2)}) collective-permute-start(f32[32,1,128]{2,0,1:T(8,128)S(1)} %get-tuple-element.33), channel_id=1, source_target_pairs={{0,16},{16,32},{32,48},{48,64},{64,80},{80,96},{96,112},{112,128},... | collective-permute-start | bytes 49160 | tf_op jit(solution)/shard_map/ppermute | solution.py:28
  244.2 2.1 all-to-all-done.7
  246.3 1.9 collective-permute-start.16
  248.2 8.1 %collective-permute-start.17 = (f32[32,1,128]{2,0,1:T(8,128)S(1)}, f32[32,1,128]{2,0,1:T(8,128)S(1)}, u32[]{:S(2)}, u32[]{:S(2)}) collective-permute-start(f32[32,1,128]{2,0,1:T(8,128)S(1)} %get-tuple-element.29), channel_id=1, source_target_pairs={{0,16},{16,32},{32,48},{48,64},{64,80},{80,96},{96,112},{112,128},... | collective-permute-start | bytes 49160 | tf_op jit(solution)/shard_map/ppermute | solution.py:28
  256.7 0.9 copy.89
  257.6 0.9 fusion.51
  258.5 0.4 fusion.70
  258.8 5.9 %collective-permute-start.18 = (f32[32,16,128]{2,0,1:T(8,128)S(1)}, f32[32,16,128]{2,0,1:T(8,128)S(1)}, u32[]{:S(2)}, u32[]{:S(2)}) collective-permute-start(f32[32,16,128]{2,0,1:T(8,128)S(1)} %fusion.70), channel_id=1, source_target_pairs={{0,16},{16,32},{32,48},{48,64},{64,80},{80,96},{96,112},{112,128},... | collective-permute-start | bytes 786440 | tf_op jit(solution)/shard_map/ppermute | solution.py:39
  264.8 0.4 fusion.68
  265.1 1.9 collective-permute-start.19
  267.4 5.8 %collective-permute-start.14 = (f32[32,16,128]{2,0,1:T(8,128)S(1)}, f32[32,16,128]{2,0,1:T(8,128)S(1)}, u32[]{:S(2)}, u32[]{:S(2)}) collective-permute-start(f32[32,16,128]{2,0,1:T(8,128)S(1)} %fusion.75), channel_id=1, source_target_pairs={{0,16},{16,32},{32,48},{48,64},{64,80},{80,96},{96,112},{112,128},... | collective-permute-start | bytes 786440 | tf_op jit(solution)/shard_map/ppermute | solution.py:39
  273.2 0.4 fusion.73
  273.5 2.1 collective-permute-start.15
  275.7 0.4 fusion
  276.4 1.9 fusion.8
  278.9 4.5 %collective-permute-done.15 = f32[32,16,128]{2,0,1:T(8,128)} collective-permute-done((f32[32,16,128]{2,0,1:T(8,128)S(1)}, f32[32,16,128]{2,0,1:T(8,128)}, u32[]{:S(2)}, u32[]{:S(2)}) %collective-permute-start.15) | collective-permute-done | bytes 262176 | tf_op jit(solution)/shard_map/ppermute | solution.py:39
  283.4 1.3 fusion.1
  285.1 1.9 fusion.10
  287.6 0.6 copy-done.2
  288.4 0.4 multiply_add_fusion
  288.8 0.9 copy.90
  289.7 0.9 copy.91
  290.5 0.9 copy.92
  (79 shorter events, 6.6 us)
Async XLA Ops:
  0.6 275.8 %copy-start = (f32[32,64,64]{2,1,0:T(8,128)S(1)}, f32[32,64,64]{2,1,0:T(8,128)}, u32[]{:S(2)}) copy-start(f32[32,64,64]{2,1,0:T(8,128)} %param.14) | copy-start | bytes 1572868
  0.6 0.7 copy-start.5
  6.2 28.0 %all-to-all-start = ((f32[32,16,256]{2,0,1:T(8,128)}), f32[32,16,256]{2,0,1:T(8,128)S(1)}, u32[]{:S(2)}, u32[]{:S(2)}) async-start(f32[32,16,256]{2,0,1:T(8,128)} %copy.68), calls=%async_computation | async-start | bytes 1048576 | tf_op jit(solution)/shard_map/all_to_all | solution.py:111
  42.8 22.0 %all-to-all-start.1 = ((f32[16,32,256]{2,1,0:T(8,128)}), f32[16,32,256]{2,1,0:T(8,128)S(1)}, u32[]{:S(2)}, u32[]{:S(2)}) async-start(f32[16,32,256]{2,1,0:T(8,128)} %fusion.14), calls=%async_computation.1 | async-start | bytes 1048576 | tf_op jit(solution)/shard_map/all_to_all | solution.py:114
  65.3 7.7 %collective-permute-start = (f32[32,1,128]{2,1,0:T(1,128)S(1)}, f32[32,1,128]{2,1,0:T(1,128)S(1)}, u32[]{:S(2)}, u32[]{:S(2)}) collective-permute-start(f32[32,1,128]{2,1,0:T(1,128)S(1)} %get-tuple-element.45), channel_id=1, source_target_pairs={{16,0},{32,16},{48,32},{64,48},{80,64},{96,80},{112,96},{128,112},... | collective-permute-start | bytes 49160 | tf_op jit(solution)/shard_map/ppermute | solution.py:31
  69.6 4.3 %collective-permute-start.1 = (f32[32,1,128]{2,1,0:T(1,128)S(1)}, f32[32,1,128]{2,1,0:T(1,128)S(1)}, u32[]{:S(2)}, u32[]{:S(2)}) collective-permute-start(f32[32,1,128]{2,1,0:T(1,128)S(1)} %get-tuple-element.46), channel_id=1, source_target_pairs={{0,16},{16,32},{32,48},{48,64},{64,80},{80,96},{96,112},{112,128},... | collective-permute-start | bytes 49160 | tf_op jit(solution)/shard_map/ppermute | solution.py:28
  74.1 8.3 %collective-permute-start.2 = (f32[32,1,128]{2,1,0:T(1,128)S(1)}, f32[32,1,128]{2,1,0:T(1,128)S(1)}, u32[]{:S(2)}, u32[]{:S(2)}) collective-permute-start(f32[32,1,128]{2,1,0:T(1,128)S(1)} %get-tuple-element.43), channel_id=1, source_target_pairs={{16,0},{32,16},{48,32},{64,48},{80,64},{96,80},{112,96},{128,112},... | collective-permute-start | bytes 49160 | tf_op jit(solution)/shard_map/ppermute | solution.py:31
  76.8 6.4 %collective-permute-start.3 = (f32[32,1,128]{2,1,0:T(1,128)S(1)}, f32[32,1,128]{2,1,0:T(1,128)S(1)}, u32[]{:S(2)}, u32[]{:S(2)}) collective-permute-start(f32[32,1,128]{2,1,0:T(1,128)S(1)} %get-tuple-element.44), channel_id=1, source_target_pairs={{0,16},{16,32},{32,48},{48,64},{64,80},{80,96},{96,112},{112,128},... | collective-permute-start | bytes 49160 | tf_op jit(solution)/shard_map/ppermute | solution.py:28
  83.4 8.3 %collective-permute-start.4 = (f32[32,1,128]{2,1,0:T(1,128)S(1)}, f32[32,1,128]{2,1,0:T(1,128)S(1)}, u32[]{:S(2)}, u32[]{:S(2)}) collective-permute-start(f32[32,1,128]{2,1,0:T(1,128)S(1)} %get-tuple-element.41), channel_id=1, source_target_pairs={{16,0},{32,16},{48,32},{64,48},{80,64},{96,80},{112,96},{128,112},... | collective-permute-start | bytes 49160 | tf_op jit(solution)/shard_map/ppermute | solution.py:31
  85.4 7.2 %collective-permute-start.5 = (f32[32,1,128]{2,1,0:T(1,128)S(1)}, f32[32,1,128]{2,1,0:T(1,128)S(1)}, u32[]{:S(2)}, u32[]{:S(2)}) collective-permute-start(f32[32,1,128]{2,1,0:T(1,128)S(1)} %get-tuple-element.42), channel_id=1, source_target_pairs={{0,16},{16,32},{32,48},{48,64},{64,80},{80,96},{96,112},{112,128},... | collective-permute-start | bytes 49160 | tf_op jit(solution)/shard_map/ppermute | solution.py:28
  93.5 15.3 %all-to-all-start.2 = ((f32[32,16,128]{2,0,1:T(8,128)}), f32[32,16,128]{2,0,1:T(8,128)S(1)}, u32[]{:S(2)}, u32[]{:S(2)}) async-start(f32[32,16,128]{2,0,1:T(8,128)} %copy.71), calls=%async_computation.2 | async-start | bytes 524288 | tf_op jit(solution)/shard_map/all_to_all | solution.py:111
  180.1 7.7 %collective-permute-start.6 = (f32[32,1,128]{2,1,0:T(1,128)S(1)}, f32[32,1,128]{2,1,0:T(1,128)S(1)}, u32[]{:S(2)}, u32[]{:S(2)}) collective-permute-start(f32[32,1,128]{2,1,0:T(1,128)S(1)} %get-tuple-element.39), channel_id=1, source_target_pairs={{16,0},{32,16},{48,32},{64,48},{80,64},{96,80},{112,96},{128,112},... | collective-permute-start | bytes 49160 | tf_op jit(solution)/shard_map/ppermute | solution.py:31
  184.6 4.0 %collective-permute-start.7 = (f32[32,1,128]{2,1,0:T(1,128)S(1)}, f32[32,1,128]{2,1,0:T(1,128)S(1)}, u32[]{:S(2)}, u32[]{:S(2)}) collective-permute-start(f32[32,1,128]{2,1,0:T(1,128)S(1)} %get-tuple-element.40), channel_id=1, source_target_pairs={{0,16},{16,32},{32,48},{48,64},{64,80},{80,96},{96,112},{112,128},... | collective-permute-start | bytes 49160 | tf_op jit(solution)/shard_map/ppermute | solution.py:28
  188.9 8.3 %collective-permute-start.8 = (f32[32,1,128]{2,1,0:T(1,128)S(1)}, f32[32,1,128]{2,1,0:T(1,128)S(1)}, u32[]{:S(2)}, u32[]{:S(2)}) collective-permute-start(f32[32,1,128]{2,1,0:T(1,128)S(1)} %get-tuple-element.37), channel_id=1, source_target_pairs={{16,0},{32,16},{48,32},{64,48},{80,64},{96,80},{112,96},{128,112},... | collective-permute-start | bytes 49160 | tf_op jit(solution)/shard_map/ppermute | solution.py:31
  191.8 6.1 %collective-permute-start.9 = (f32[32,1,128]{2,1,0:T(1,128)S(1)}, f32[32,1,128]{2,1,0:T(1,128)S(1)}, u32[]{:S(2)}, u32[]{:S(2)}) collective-permute-start(f32[32,1,128]{2,1,0:T(1,128)S(1)} %get-tuple-element.38), channel_id=1, source_target_pairs={{0,16},{16,32},{32,48},{48,64},{64,80},{80,96},{96,112},{112,128},... | collective-permute-start | bytes 49160 | tf_op jit(solution)/shard_map/ppermute | solution.py:28
  198.2 8.3 %collective-permute-start.10 = (f32[32,1,128]{2,1,0:T(1,128)S(1)}, f32[32,1,128]{2,1,0:T(1,128)S(1)}, u32[]{:S(2)}, u32[]{:S(2)}) collective-permute-start(f32[32,1,128]{2,1,0:T(1,128)S(1)} %get-tuple-element.35), channel_id=1, source_target_pairs={{16,0},{32,16},{48,32},{64,48},{80,64},{96,80},{112,96},{128,112},... | collective-permute-start | bytes 49160 | tf_op jit(solution)/shard_map/ppermute | solution.py:31
  200.1 7.2 %collective-permute-start.11 = (f32[32,1,128]{2,1,0:T(1,128)S(1)}, f32[32,1,128]{2,1,0:T(1,128)S(1)}, u32[]{:S(2)}, u32[]{:S(2)}) collective-permute-start(f32[32,1,128]{2,1,0:T(1,128)S(1)} %get-tuple-element.36), channel_id=1, source_target_pairs={{0,16},{16,32},{32,48},{48,64},{64,80},{80,96},{96,112},{112,128},... | collective-permute-start | bytes 49160 | tf_op jit(solution)/shard_map/ppermute | solution.py:28
  208.3 4.3 %copy-start.7 = (s32[2,32,1]{1,2,0:T(1,128)S(1)}, s32[2,32,1]{1,2,0:T(1,128)}, u32[]{:S(2)}) copy-start(s32[2,32,1]{1,2,0:T(1,128)} %param.15) | copy-start | bytes 772
  208.3 15.4 %all-to-all-start.6 = ((f32[32,16,128]{2,0,1:T(8,128)}), f32[32,16,128]{2,0,1:T(8,128)S(1)}, u32[]{:S(2)}, u32[]{:S(2)}) async-start(f32[32,16,128]{2,0,1:T(8,128)} %copy.77), calls=%async_computation.6 | async-start | bytes 524288 | tf_op jit(solution)/shard_map/all_to_all | solution.py:111
  230.5 3.7 %copy-start.6 = (s32[2,32,1]{1,2,0:T(1,128)S(1)}, s32[2,32,1]{1,2,0:T(1,128)}, u32[]{:S(2)}) copy-start(s32[2,32,1]{1,2,0:T(1,128)} %param.16) | copy-start | bytes 772
  230.5 15.8 %all-to-all-start.7 = ((f32[16,32,128]{2,1,0:T(8,128)}), f32[16,32,128]{2,1,0:T(8,128)S(1)}, u32[]{:S(2)}, u32[]{:S(2)}) async-start(f32[16,32,128]{2,1,0:T(8,128)} %fusion.21), calls=%async_computation.7 | async-start | bytes 524288 | tf_op jit(solution)/shard_map/all_to_all | solution.py:114
  234.2 23.3 %collective-permute-start.12 = (f32[32,1,128]{2,0,1:T(8,128)S(1)}, f32[32,1,128]{2,0,1:T(8,128)S(1)}, u32[]{:S(2)}, u32[]{:S(2)}) collective-permute-start(f32[32,1,128]{2,0,1:T(8,128)S(1)} %get-tuple-element.34), channel_id=1, source_target_pairs={{16,0},{32,16},{48,32},{64,48},{80,64},{96,80},{112,96},{128,112},... | collective-permute-start | bytes 49160 | tf_op jit(solution)/shard_map/ppermute | solution.py:31
  236.1 20.2 %copy-start.1 = (f32[32,16,128]{2,1,0:T(8,128)S(1)}, f32[32,16,128]{2,1,0:T(8,128)}, u32[]{:S(2)}) copy-start(f32[32,16,128]{2,1,0:T(8,128)} %param.13) | copy-start | bytes 786436
  236.2 21.4 %collective-permute-start.13 = (f32[32,1,128]{2,0,1:T(8,128)S(1)}, f32[32,1,128]{2,0,1:T(8,128)S(1)}, u32[]{:S(2)}, u32[]{:S(2)}) collective-permute-start(f32[32,1,128]{2,0,1:T(8,128)S(1)} %get-tuple-element.33), channel_id=1, source_target_pairs={{0,16},{16,32},{32,48},{48,64},{64,80},{80,96},{96,112},{112,128},... | collective-permute-start | bytes 49160 | tf_op jit(solution)/shard_map/ppermute | solution.py:28
  246.3 11.3 %collective-permute-start.16 = (f32[32,1,128]{2,0,1:T(8,128)S(1)}, f32[32,1,128]{2,0,1:T(8,128)S(1)}, u32[]{:S(2)}, u32[]{:S(2)}) collective-permute-start(f32[32,1,128]{2,0,1:T(8,128)S(1)} %get-tuple-element.30), channel_id=1, source_target_pairs={{16,0},{32,16},{48,32},{64,48},{80,64},{96,80},{112,96},{128,112},... | collective-permute-start | bytes 49160 | tf_op jit(solution)/shard_map/ppermute | solution.py:31
  248.2 9.3 %collective-permute-start.17 = (f32[32,1,128]{2,0,1:T(8,128)S(1)}, f32[32,1,128]{2,0,1:T(8,128)S(1)}, u32[]{:S(2)}, u32[]{:S(2)}) collective-permute-start(f32[32,1,128]{2,0,1:T(8,128)S(1)} %get-tuple-element.29), channel_id=1, source_target_pairs={{0,16},{16,32},{32,48},{48,64},{64,80},{80,96},{96,112},{112,128},... | collective-permute-start | bytes 49160 | tf_op jit(solution)/shard_map/ppermute | solution.py:28
  258.8 16.9 %collective-permute-start.18 = (f32[32,16,128]{2,0,1:T(8,128)S(1)}, f32[32,16,128]{2,0,1:T(8,128)S(1)}, u32[]{:S(2)}, u32[]{:S(2)}) collective-permute-start(f32[32,16,128]{2,0,1:T(8,128)S(1)} %fusion.70), channel_id=1, source_target_pairs={{0,16},{16,32},{32,48},{48,64},{64,80},{80,96},{96,112},{112,128},... | collective-permute-start | bytes 786440 | tf_op jit(solution)/shard_map/ppermute | solution.py:39
  265.1 10.6 %collective-permute-start.19 = (f32[32,16,128]{2,0,1:T(8,128)S(1)}, f32[32,16,128]{2,0,1:T(8,128)S(1)}, u32[]{:S(2)}, u32[]{:S(2)}) collective-permute-start(f32[32,16,128]{2,0,1:T(8,128)S(1)} %fusion.68), channel_id=1, source_target_pairs={{16,0},{32,16},{48,32},{64,48},{80,64},{96,80},{112,96},{128,112},... | collective-permute-start | bytes 786440 | tf_op jit(solution)/shard_map/ppermute | solution.py:39
  267.4 11.5 %collective-permute-start.14 = (f32[32,16,128]{2,0,1:T(8,128)S(1)}, f32[32,16,128]{2,0,1:T(8,128)S(1)}, u32[]{:S(2)}, u32[]{:S(2)}) collective-permute-start(f32[32,16,128]{2,0,1:T(8,128)S(1)} %fusion.75), channel_id=1, source_target_pairs={{0,16},{16,32},{32,48},{48,64},{64,80},{80,96},{96,112},{112,128},... | collective-permute-start | bytes 786440 | tf_op jit(solution)/shard_map/ppermute | solution.py:39
  273.5 9.9 %collective-permute-start.15 = (f32[32,16,128]{2,0,1:T(8,128)S(1)}, f32[32,16,128]{2,0,1:T(8,128)}, u32[]{:S(2)}, u32[]{:S(2)}) collective-permute-start(f32[32,16,128]{2,0,1:T(8,128)S(1)} %fusion.73), channel_id=1, source_target_pairs={{16,0},{32,16},{48,32},{64,48},{80,64},{96,80},{112,96},{128,112},... | collective-permute-start | bytes 786440 | tf_op jit(solution)/shard_map/ppermute | solution.py:39
  287.3 1.0 copy-start.2
  287.3 1.0 copy-start.3
  287.3 1.1 copy-start.4
where the time goes:
time: 293 us; the launch traced here: 291 us
  starting transfers between devices  111 us (38%)
  waiting for transfers between devices  68.2 us (23%)
  blocking collectives  56.9 us (19%)
  matrix products  35.4 us (12%)
  local copies, waits for them, and re-layouts  12.6 us (4%)
  other arithmetic  5.6 us (2%)
    ppermute x8, starting transfers between devices, with_halo(): lax.ppermute(lax.slice_in_dim(block, block.shape[dim] - width, None, axis...  45.9 us
    all_to_all x3, waiting for transfers between devices, transform(): lax.all_to_all(columns_all, 'azim', split_axis=1, concat_axis=0, tiled=True)  39.3 us
    all_to_all x2, blocking collectives, transform(): lax.all_to_all(mixed, 'azim', split_axis=0, concat_axis=1, tiled=True)  35.2 us
    dot_general x4, matrix products, transform(): jnp.dot(full_table.T, spread, precision=HIGH, preferred_element_type=jnp....  28.5 us
    ppermute x8, starting transfers between devices, with_halo(): lax.ppermute(lax.slice_in_dim(block, 0, width, axis=dim), axis, backward)  22.1 us
    all_to_all x1, blocking collectives, transform(): lax.all_to_all(columns_all, 'azim', split_axis=1, concat_axis=0, tiled=True)  21.7 us
    all_to_all x2, waiting for transfers between devices, transform(): lax.all_to_all(mixed, 'azim', split_axis=0, concat_axis=1, tiled=True)  19.3 us
    all_to_all x3, starting transfers between devices, transform(): lax.all_to_all(columns_all, 'azim', split_axis=1, concat_axis=0, tiled=True)  19.2 us
  transfers between devices with their start and end apart: 25, of which 12 were waited for; matrix products, arithmetic and copies ran while one was open for 2% of the time, Pallas kernels for 0%

commit v1 on v0

--- a/solution.py
+++ b/solution.py
@@ -108,7 +108,12 @@
 def transform(parts, table_rows, all_index):
     flat_shape = parts.shape
     columns_all = parts.reshape(flat_shape[0], -1)
-    spread = lax.all_to_all(columns_all, "azim", split_axis=1, concat_axis=0, tiled=True)
+    spread = jnp.concatenate(
+        lax.all_to_all(
+            jnp.stack(jnp.split(columns_all, lax.axis_size("azim"), axis=1)), "azim", 0, 0
+        ),
+        axis=0,
+    )
     full_table = table_rows(all_index, all_index)
     mixed = jnp.dot(full_table.T, spread, precision=HIGH, preferred_element_type=jnp.float32)
     joined = lax.all_to_all(mixed, "azim", split_axis=0, concat_axis=1, tiled=True)

time: 293 us -> 320 us (1.092)
  local copies, waits for them, and re-layouts: 12.6 us -> 39.3 us
    unnamed x20 -> x84, local copies, waits for them, and re-layouts: 4.97 us -> 33.1 us
where the time goes in v1:
time: 320 us; the launch traced here: 318 us
  starting transfers between devices  111 us (35%)
  waiting for transfers between devices  68.2 us (21%)
  blocking collectives  56.9 us (18%)
  local copies, waits for them, and re-layouts  39.3 us (12%)
  matrix products  35.4 us (11%)
  other arithmetic  5.6 us (2%)
    ppermute x8, starting transfers between devices, with_halo(): lax.ppermute(lax.slice_in_dim(block, block.shape[dim] - width, None, axis...  46 us
    all_to_all x3, waiting for transfers between devices, transform(): lax.all_to_all(jnp.stack(jnp.split(columns_all, lax.axis_size('azim'), ax...  39.3 us
    all_to_all x2, blocking collectives, transform(): lax.all_to_all(mixed, 'azim', split_axis=0, concat_axis=1, tiled=True)  35.2 us
    unnamed x84, local copies, waits for them, and re-layouts  33.1 us
    dot_general x4, matrix products, transform(): jnp.dot(full_table.T, spread, precision=HIGH, preferred_element_type=jnp....  28.5 us
    ppermute x8, starting transfers between devices, with_halo(): lax.ppermute(lax.slice_in_dim(block, 0, width, axis=dim), axis, backward)  22.1 us
    all_to_all x1, blocking collectives, transform(): lax.all_to_all(jnp.stack(jnp.split(columns_all, lax.axis_size('azim'), ax...  21.7 us
    all_to_all x2, waiting for transfers between devices, transform(): lax.all_to_all(mixed, 'azim', split_axis=0, concat_axis=1, tiled=True)  19.3 us
  transfers between devices with their start and end apart: 25, of which 12 were waited for; matrix products, arithmetic and copies ran while one was open for 2% of the time, Pallas kernels for 0%

profile of v1, /device:TPU:25, one launch (start us, length us, event | category | flops | bytes accessed | tf_op | source)
XLA Modules:
  0.0 318.3 jit_solution(3733252265822538703)
XLA Ops:
  0.7 0.7 copy-done.5
  2.0 2.6 multiply_bitcast_fusion.1
  6.5 0.6 constant_dynamic-update-slice_fusion.13
  8.3 0.6 constant_dynamic-update-slice_fusion.10
  8.9 0.6 constant_dynamic-update-slice_fusion.9
  10.8 0.6 constant_dynamic-update-slice_fusion.6
  12.0 0.6 constant_dynamic-update-slice_fusion.4
  15.0 10.7 %all-to-all-start = ((f32[16,32,256]{2,1,0:T(8,128)}), f32[16,32,256]{2,1,0:T(8,128)S(1)}, u32[]{:S(2)}, u32[]{:S(2)}) async-start(f32[16,32,256]{2,1,0:T(8,128)} %constant_dynamic-update-slice_fusion), calls=%async_computation | async-start | bytes 1048576 | tf_op jit(solution)/shard_map/all_to_all | solution.py:112
  25.8 17.2 %all-to-all-done = f32[16,32,256]{2,1,0:T(8,128)S(1)} async-done(((f32[16,32,256]{2,1,0:T(8,128)}), f32[16,32,256]{2,1,0:T(8,128)S(1)}, u32[]{:S(2)}, u32[]{:S(2)}) %all-to-all-start) | async-done | bytes 524320 | tf_op jit(solution)/shard_map/all_to_all | solution.py:112
  43.0 8.6 %fusion.14 = f32[16,32,256]{2,1,0:T(8,128)} fusion(f32[512,256,1]{1,0,2:T(8,128)S(1)} %bitcast.469, s32[16,32]{1,0:T(8,128)S(1)} %add_select_fusion.2, pred[16,32]{1,0:T(8,128)(4,1)S(1)} %fusion.99), kind=kOutput, calls=%fused_computation.24 | convolution fusion | flops 809238528 | bytes 1051136 | tf_op jit(solution)/shard_map/dot_general | solution.py:118
  51.6 4.7 %all-to-all-start.1 = ((f32[16,32,256]{2,1,0:T(8,128)}), f32[16,32,256]{2,1,0:T(8,128)S(1)}, u32[]{:S(2)}, u32[]{:S(2)}) async-start(f32[16,32,256]{2,1,0:T(8,128)} %fusion.14), calls=%async_computation.1 | async-start | bytes 1048576 | tf_op jit(solution)/shard_map/all_to_all | solution.py:119
  56.4 17.2 %all-to-all-done.1 = f32[16,32,256]{2,1,0:T(8,128)S(1)} async-done(((f32[16,32,256]{2,1,0:T(8,128)}), f32[16,32,256]{2,1,0:T(8,128)S(1)}, u32[]{:S(2)}, u32[]{:S(2)}) %all-to-all-start.1) | async-done | bytes 524320 | tf_op jit(solution)/shard_map/all_to_all | solution.py:119
  74.1 4.3 %collective-permute-start = (f32[32,1,128]{2,1,0:T(1,128)S(1)}, f32[32,1,128]{2,1,0:T(1,128)S(1)}, u32[]{:S(2)}, u32[]{:S(2)}) collective-permute-start(f32[32,1,128]{2,1,0:T(1,128)S(1)} %get-tuple-element.41), channel_id=1, source_target_pairs={{16,0},{32,16},{48,32},{64,48},{80,64},{96,80},{112,96},{128,112},... | collective-permute-start | bytes 49160 | tf_op jit(solution)/shard_map/ppermute | solution.py:31
  78.3 3.4 %collective-permute-start.1 = (f32[32,1,128]{2,1,0:T(1,128)S(1)}, f32[32,1,128]{2,1,0:T(1,128)S(1)}, u32[]{:S(2)}, u32[]{:S(2)}) collective-permute-start(f32[32,1,128]{2,1,0:T(1,128)S(1)} %get-tuple-element.42), channel_id=1, source_target_pairs={{0,16},{16,32},{32,48},{48,64},{64,80},{80,96},{96,112},{112,128},... | collective-permute-start | bytes 49160 | tf_op jit(solution)/shard_map/ppermute | solution.py:28
  81.8 0.8 collective-permute-done.1
  82.9 2.7 collective-permute-start.2
  85.6 5.5 %collective-permute-start.3 = (f32[32,1,128]{2,1,0:T(1,128)S(1)}, f32[32,1,128]{2,1,0:T(1,128)S(1)}, u32[]{:S(2)}, u32[]{:S(2)}) collective-permute-start(f32[32,1,128]{2,1,0:T(1,128)S(1)} %get-tuple-element.40), channel_id=1, source_target_pairs={{0,16},{16,32},{32,48},{48,64},{64,80},{80,96},{96,112},{112,128},... | collective-permute-start | bytes 49160 | tf_op jit(solution)/shard_map/ppermute | solution.py:28
  91.1 0.8 collective-permute-done.3
  92.2 1.9 collective-permute-start.4
  94.1 6.3 %collective-permute-start.5 = (f32[32,1,128]{2,1,0:T(1,128)S(1)}, f32[32,1,128]{2,1,0:T(1,128)S(1)}, u32[]{:S(2)}, u32[]{:S(2)}) collective-permute-start(f32[32,1,128]{2,1,0:T(1,128)S(1)} %get-tuple-element.38), channel_id=1, source_target_pairs={{0,16},{16,32},{32,48},{48,64},{64,80},{80,96},{96,112},{112,128},... | collective-permute-start | bytes 49160 | tf_op jit(solution)/shard_map/ppermute | solution.py:28
  100.5 0.8 collective-permute-done.5
  101.6 0.6 constant_dynamic-update-slice_fusion.31
  102.2 0.6 constant_dynamic-update-slice_fusion.30
  104.6 0.6 constant_dynamic-update-slice_fusion.26
  111.3 4.2 %all-to-all-start.2 = ((f32[16,32,128]{2,1,0:T(8,128)}), f32[16,32,128]{2,1,0:T(8,128)S(1)}, u32[]{:S(2)}, u32[]{:S(2)}) async-start(f32[16,32,128]{2,1,0:T(8,128)} %constant_dynamic-update-slice_fusion.16), calls=%async_computation.2 | async-start | bytes 524288 | tf_op jit(solution)/shard_map/all_to_all | solution.py:112
  115.5 11.1 %all-to-all-done.2 = f32[16,32,128]{2,1,0:T(8,128)S(1)} async-done(((f32[16,32,128]{2,1,0:T(8,128)}), f32[16,32,128]{2,1,0:T(8,128)S(1)}, u32[]{:S(2)}, u32[]{:S(2)}) %all-to-all-start.2) | async-done | bytes 262176 | tf_op jit(solution)/shard_map/all_to_all | solution.py:112
  126.6 5.1 %fusion.22 = f32[16,32,128]{2,1,0:T(8,128)S(1)} fusion(f32[512,128,1]{1,0,2:T(8,128)S(1)} %bitcast.472, f32[512]{0:T(512)S(1)} %fusion.101, s32[512]{0:T(512)S(1)} %add_select_fusion.3, s32[16,32]{1,0:T(8,128)S(1)} %multiply_add_fusion.3, pred[512]{0:T(512)(128)(4,1)S(1)} %iota_compare_fusion.4), kind=kOutput, calls=%fused_computation.54 | convolution fusion | flops 406847488 | bytes 530944 | tf_op jit(solution)/shard_map/dot_general | solution.py:118
  131.7 14.8 %all_to_all.72 = f32[16,32,128]{2,1,0:T(8,128)S(1)} all-to-all(f32[16,32,128]{2,1,0:T(8,128)S(1)} %fusion.22), channel_id=1, replica_groups=mesh['axial'=16,'azim'=16] {'azim'}, dimensions={0} | all-to-all | bytes 524288 | tf_op jit(solution)/shard_map/all_to_all | solution.py:119
  147.4 21.7 %all_to_all.73 = f32[16,32,256]{2,1,0:T(8,128)S(1)} all-to-all(f32[16,32,256]{2,1,0:T(8,128)S(1)} %constant_dynamic-update-slice_fusion.32), channel_id=1, replica_groups=mesh['axial'=16,'azim'=16] {'azim'}, dimensions={0} | all-to-all | bytes 1048576 | tf_op jit(solution)/shard_map/all_to_all | solution.py:112
  169.1 8.0 %fusion.12 = f32[16,32,256]{2,1,0:T(8,128)S(1)} fusion(f32[512,256,1]{1,0,2:T(8,128)S(1)} %bitcast.470, s32[16,32]{1,0:T(8,128)S(1)} %add_select_fusion.2, pred[16,32]{1,0:T(8,128)(4,1)S(1)} %fusion.99), kind=kOutput, calls=%fused_computation.22 | convolution fusion | flops 809238528 | bytes 1051136 | tf_op jit(solution)/shard_map/dot_general | solution.py:118
  177.1 20.4 %all_to_all.74 = f32[16,32,256]{2,1,0:T(8,128)S(1)} all-to-all(f32[16,32,256]{2,1,0:T(8,128)S(1)} %fusion.12), channel_id=1, replica_groups=mesh['axial'=16,'azim'=16] {'azim'}, dimensions={0} | all-to-all | bytes 1048576 | tf_op jit(solution)/shard_map/all_to_all | solution.py:119
  197.9 4.5 %collective-permute-start.6 = (f32[32,1,128]{2,1,0:T(1,128)S(1)}, f32[32,1,128]{2,1,0:T(1,128)S(1)}, u32[]{:S(2)}, u32[]{:S(2)}) collective-permute-start(f32[32,1,128]{2,1,0:T(1,128)S(1)} %get-tuple-element.35), channel_id=1, source_target_pairs={{16,0},{32,16},{48,32},{64,48},{80,64},{96,80},{112,96},{128,112},... | collective-permute-start | bytes 49160 | tf_op jit(solution)/shard_map/ppermute | solution.py:31
  202.4 3.2 collective-permute-start.7
  205.6 0.8 collective-permute-done.7
  206.7 3.0 collective-permute-start.8
  209.7 5.3 %collective-permute-start.9 = (f32[32,1,128]{2,1,0:T(1,128)S(1)}, f32[32,1,128]{2,1,0:T(1,128)S(1)}, u32[]{:S(2)}, u32[]{:S(2)}) collective-permute-start(f32[32,1,128]{2,1,0:T(1,128)S(1)} %get-tuple-element.34), channel_id=1, source_target_pairs={{0,16},{16,32},{32,48},{48,64},{64,80},{80,96},{96,112},{112,128},... | collective-permute-start | bytes 49160 | tf_op jit(solution)/shard_map/ppermute | solution.py:28
  215.0 0.8 collective-permute-done.9
  216.0 1.9 collective-permute-start.10
  218.0 6.3 %collective-permute-start.11 = (f32[32,1,128]{2,1,0:T(1,128)S(1)}, f32[32,1,128]{2,1,0:T(1,128)S(1)}, u32[]{:S(2)}, u32[]{:S(2)}) collective-permute-start(f32[32,1,128]{2,1,0:T(1,128)S(1)} %get-tuple-element.32), channel_id=1, source_target_pairs={{0,16},{16,32},{32,48},{48,64},{64,80},{80,96},{96,112},{112,128},... | collective-permute-start | bytes 49160 | tf_op jit(solution)/shard_map/ppermute | solution.py:28
  224.3 0.8 collective-permute-done.11
  225.5 0.6 constant_dynamic-update-slice_fusion.63
  235.2 4.2 %all-to-all-start.6 = ((f32[16,32,128]{2,1,0:T(8,128)}), f32[16,32,128]{2,1,0:T(8,128)S(1)}, u32[]{:S(2)}, u32[]{:S(2)}) async-start(f32[16,32,128]{2,1,0:T(8,128)} %constant_dynamic-update-slice_fusion.48), calls=%async_computation.6 | async-start | bytes 524288 | tf_op jit(solution)/shard_map/all_to_all | solution.py:112
  239.5 11.1 %all-to-all-done.6 = f32[16,32,128]{2,1,0:T(8,128)S(1)} async-done(((f32[16,32,128]{2,1,0:T(8,128)}), f32[16,32,128]{2,1,0:T(8,128)S(1)}, u32[]{:S(2)}, u32[]{:S(2)}) %all-to-all-start.6) | async-done | bytes 262176 | tf_op jit(solution)/shard_map/all_to_all | solution.py:112
  250.6 6.8 %fusion.21 = f32[16,32,128]{2,1,0:T(8,128)} fusion(f32[512,128,1]{1,0,2:T(8,128)S(1)} %bitcast.471, f32[512]{0:T(512)S(1)} %fusion.101, s32[512]{0:T(512)S(1)} %add_select_fusion.3, s32[16,32]{1,0:T(8,128)S(1)} %multiply_add_fusion.3, pred[512]{0:T(512)(128)(4,1)S(1)} %iota_compare_fusion.4), kind=kOutput, calls=%fused_computation.53 | convolution fusion | flops 406847488 | bytes 530944 | tf_op jit(solution)/shard_map/dot_general | solution.py:118
  257.3 3.7 %all-to-all-start.7 = ((f32[16,32,128]{2,1,0:T(8,128)}), f32[16,32,128]{2,1,0:T(8,128)S(1)}, u32[]{:S(2)}, u32[]{:S(2)}) async-start(f32[16,32,128]{2,1,0:T(8,128)} %fusion.21), calls=%async_computation.7 | async-start | bytes 524288 | tf_op jit(solution)/shard_map/all_to_all | solution.py:119
  261.1 1.9 collective-permute-start.12
  263.0 7.9 %collective-permute-start.13 = (f32[32,1,128]{2,0,1:T(8,128)S(1)}, f32[32,1,128]{2,0,1:T(8,128)S(1)}, u32[]{:S(2)}, u32[]{:S(2)}) collective-permute-start(f32[32,1,128]{2,0,1:T(8,128)S(1)} %get-tuple-element.29), channel_id=1, source_target_pairs={{0,16},{16,32},{32,48},{48,64},{64,80},{80,96},{96,112},{112,128},... | collective-permute-start | bytes 49160 | tf_op jit(solution)/shard_map/ppermute | solution.py:28
  271.1 2.1 all-to-all-done.7
  273.2 1.9 collective-permute-start.16
  275.1 8.1 %collective-permute-start.17 = (f32[32,1,128]{2,0,1:T(8,128)S(1)}, f32[32,1,128]{2,0,1:T(8,128)S(1)}, u32[]{:S(2)}, u32[]{:S(2)}) collective-permute-start(f32[32,1,128]{2,0,1:T(8,128)S(1)} %get-tuple-element.25), channel_id=1, source_target_pairs={{0,16},{16,32},{32,48},{48,64},{64,80},{80,96},{96,112},{112,128},... | collective-permute-start | bytes 49160 | tf_op jit(solution)/shard_map/ppermute | solution.py:28
  283.6 0.9 copy.55
  284.4 0.9 fusion.51
  285.7 5.9 %collective-permute-start.18 = (f32[32,16,128]{2,0,1:T(8,128)S(1)}, f32[32,16,128]{2,0,1:T(8,128)S(1)}, u32[]{:S(2)}, u32[]{:S(2)}) collective-permute-start(f32[32,16,128]{2,0,1:T(8,128)S(1)} %fusion.70), channel_id=1, source_target_pairs={{0,16},{16,32},{32,48},{48,64},{64,80},{80,96},{96,112},{112,128},... | collective-permute-start | bytes 786440 | tf_op jit(solution)/shard_map/ppermute | solution.py:39
  292.0 1.9 collective-permute-start.19
  294.3 5.8 %collective-permute-start.14 = (f32[32,16,128]{2,0,1:T(8,128)S(1)}, f32[32,16,128]{2,0,1:T(8,128)S(1)}, u32[]{:S(2)}, u32[]{:S(2)}) collective-permute-start(f32[32,16,128]{2,0,1:T(8,128)S(1)} %fusion.75), channel_id=1, source_target_pairs={{0,16},{16,32},{32,48},{48,64},{64,80},{80,96},{96,112},{112,128},... | collective-permute-start | bytes 786440 | tf_op jit(solution)/shard_map/ppermute | solution.py:39
  300.4 2.1 collective-permute-start.15
  303.3 1.9 fusion.8
  305.8 4.5 %collective-permute-done.15 = f32[32,16,128]{2,0,1:T(8,128)} collective-permute-done((f32[32,16,128]{2,0,1:T(8,128)S(1)}, f32[32,16,128]{2,0,1:T(8,128)}, u32[]{:S(2)}, u32[]{:S(2)}) %collective-permute-start.15) | collective-permute-done | bytes 262176 | tf_op jit(solution)/shard_map/ppermute | solution.py:39
  310.3 1.3 fusion.1
  311.9 1.9 fusion.10
  314.5 0.6 copy-done.2
  315.7 0.9 copy.56
  316.5 0.9 copy.57
  317.4 0.9 copy.58
  (141 shorter events, 32.9 us)
Async XLA Ops:
  0.6 302.6 %copy-start = (f32[32,64,64]{2,1,0:T(8,128)S(1)}, f32[32,64,64]{2,1,0:T(8,128)}, u32[]{:S(2)}) copy-start(f32[32,64,64]{2,1,0:T(8,128)} %param.14) | copy-start | bytes 1572868
  0.6 0.7 copy-start.5
  15.0 28.0 %all-to-all-start = ((f32[16,32,256]{2,1,0:T(8,128)}), f32[16,32,256]{2,1,0:T(8,128)S(1)}, u32[]{:S(2)}, u32[]{:S(2)}) async-start(f32[16,32,256]{2,1,0:T(8,128)} %constant_dynamic-update-slice_fusion), calls=%async_computation | async-start | bytes 1048576 | tf_op jit(solution)/shard_map/all_to_all | solution.py:112
  51.6 22.1 %all-to-all-start.1 = ((f32[16,32,256]{2,1,0:T(8,128)}), f32[16,32,256]{2,1,0:T(8,128)S(1)}, u32[]{:S(2)}, u32[]{:S(2)}) async-start(f32[16,32,256]{2,1,0:T(8,128)} %fusion.14), calls=%async_computation.1 | async-start | bytes 1048576 | tf_op jit(solution)/shard_map/all_to_all | solution.py:119
  74.1 7.7 %collective-permute-start = (f32[32,1,128]{2,1,0:T(1,128)S(1)}, f32[32,1,128]{2,1,0:T(1,128)S(1)}, u32[]{:S(2)}, u32[]{:S(2)}) collective-permute-start(f32[32,1,128]{2,1,0:T(1,128)S(1)} %get-tuple-element.41), channel_id=1, source_target_pairs={{16,0},{32,16},{48,32},{64,48},{80,64},{96,80},{112,96},{128,112},... | collective-permute-start | bytes 49160 | tf_op jit(solution)/shard_map/ppermute | solution.py:31
  78.3 4.3 %collective-permute-start.1 = (f32[32,1,128]{2,1,0:T(1,128)S(1)}, f32[32,1,128]{2,1,0:T(1,128)S(1)}, u32[]{:S(2)}, u32[]{:S(2)}) collective-permute-start(f32[32,1,128]{2,1,0:T(1,128)S(1)} %get-tuple-element.42), channel_id=1, source_target_pairs={{0,16},{16,32},{32,48},{48,64},{64,80},{80,96},{96,112},{112,128},... | collective-permute-start | bytes 49160 | tf_op jit(solution)/shard_map/ppermute | solution.py:28
  82.9 8.3 %collective-permute-start.2 = (f32[32,1,128]{2,1,0:T(1,128)S(1)}, f32[32,1,128]{2,1,0:T(1,128)S(1)}, u32[]{:S(2)}, u32[]{:S(2)}) collective-permute-start(f32[32,1,128]{2,1,0:T(1,128)S(1)} %get-tuple-element.39), channel_id=1, source_target_pairs={{16,0},{32,16},{48,32},{64,48},{80,64},{96,80},{112,96},{128,112},... | collective-permute-start | bytes 49160 | tf_op jit(solution)/shard_map/ppermute | solution.py:31
  85.6 6.4 %collective-permute-start.3 = (f32[32,1,128]{2,1,0:T(1,128)S(1)}, f32[32,1,128]{2,1,0:T(1,128)S(1)}, u32[]{:S(2)}, u32[]{:S(2)}) collective-permute-start(f32[32,1,128]{2,1,0:T(1,128)S(1)} %get-tuple-element.40), channel_id=1, source_target_pairs={{0,16},{16,32},{32,48},{48,64},{64,80},{80,96},{96,112},{112,128},... | collective-permute-start | bytes 49160 | tf_op jit(solution)/shard_map/ppermute | solution.py:28
  92.2 8.3 %collective-permute-start.4 = (f32[32,1,128]{2,1,0:T(1,128)S(1)}, f32[32,1,128]{2,1,0:T(1,128)S(1)}, u32[]{:S(2)}, u32[]{:S(2)}) collective-permute-start(f32[32,1,128]{2,1,0:T(1,128)S(1)} %get-tuple-element.37), channel_id=1, source_target_pairs={{16,0},{32,16},{48,32},{64,48},{80,64},{96,80},{112,96},{128,112},... | collective-permute-start | bytes 49160 | tf_op jit(solution)/shard_map/ppermute | solution.py:31
  94.1 7.2 %collective-permute-start.5 = (f32[32,1,128]{2,1,0:T(1,128)S(1)}, f32[32,1,128]{2,1,0:T(1,128)S(1)}, u32[]{:S(2)}, u32[]{:S(2)}) collective-permute-start(f32[32,1,128]{2,1,0:T(1,128)S(1)} %get-tuple-element.38), channel_id=1, source_target_pairs={{0,16},{16,32},{32,48},{48,64},{64,80},{80,96},{96,112},{112,128},... | collective-permute-start | bytes 49160 | tf_op jit(solution)/shard_map/ppermute | solution.py:28
  111.3 15.3 %all-to-all-start.2 = ((f32[16,32,128]{2,1,0:T(8,128)}), f32[16,32,128]{2,1,0:T(8,128)S(1)}, u32[]{:S(2)}, u32[]{:S(2)}) async-start(f32[16,32,128]{2,1,0:T(8,128)} %constant_dynamic-update-slice_fusion.16), calls=%async_computation.2 | async-start | bytes 524288 | tf_op jit(solution)/shard_map/all_to_all | solution.py:112
  197.9 7.7 %collective-permute-start.6 = (f32[32,1,128]{2,1,0:T(1,128)S(1)}, f32[32,1,128]{2,1,0:T(1,128)S(1)}, u32[]{:S(2)}, u32[]{:S(2)}) collective-permute-start(f32[32,1,128]{2,1,0:T(1,128)S(1)} %get-tuple-element.35), channel_id=1, source_target_pairs={{16,0},{32,16},{48,32},{64,48},{80,64},{96,80},{112,96},{128,112},... | collective-permute-start | bytes 49160 | tf_op jit(solution)/shard_map/ppermute | solution.py:31
  202.4 4.0 %collective-permute-start.7 = (f32[32,1,128]{2,1,0:T(1,128)S(1)}, f32[32,1,128]{2,1,0:T(1,128)S(1)}, u32[]{:S(2)}, u32[]{:S(2)}) collective-permute-start(f32[32,1,128]{2,1,0:T(1,128)S(1)} %get-tuple-element.36), channel_id=1, source_target_pairs={{0,16},{16,32},{32,48},{48,64},{64,80},{80,96},{96,112},{112,128},... | collective-permute-start | bytes 49160 | tf_op jit(solution)/shard_map/ppermute | solution.py:28
  206.7 8.3 %collective-permute-start.8 = (f32[32,1,128]{2,1,0:T(1,128)S(1)}, f32[32,1,128]{2,1,0:T(1,128)S(1)}, u32[]{:S(2)}, u32[]{:S(2)}) collective-permute-start(f32[32,1,128]{2,1,0:T(1,128)S(1)} %get-tuple-element.33), channel_id=1, source_target_pairs={{16,0},{32,16},{48,32},{64,48},{80,64},{96,80},{112,96},{128,112},... | collective-permute-start | bytes 49160 | tf_op jit(solution)/shard_map/ppermute | solution.py:31
  209.7 6.1 %collective-permute-start.9 = (f32[32,1,128]{2,1,0:T(1,128)S(1)}, f32[32,1,128]{2,1,0:T(1,128)S(1)}, u32[]{:S(2)}, u32[]{:S(2)}) collective-permute-start(f32[32,1,128]{2,1,0:T(1,128)S(1)} %get-tuple-element.34), channel_id=1, source_target_pairs={{0,16},{16,32},{32,48},{48,64},{64,80},{80,96},{96,112},{112,128},... | collective-permute-start | bytes 49160 | tf_op jit(solution)/shard_map/ppermute | solution.py:28
  216.0 8.3 %collective-permute-start.10 = (f32[32,1,128]{2,1,0:T(1,128)S(1)}, f32[32,1,128]{2,1,0:T(1,128)S(1)}, u32[]{:S(2)}, u32[]{:S(2)}) collective-permute-start(f32[32,1,128]{2,1,0:T(1,128)S(1)} %get-tuple-element.31), channel_id=1, source_target_pairs={{16,0},{32,16},{48,32},{64,48},{80,64},{96,80},{112,96},{128,112},... | collective-permute-start | bytes 49160 | tf_op jit(solution)/shard_map/ppermute | solution.py:31
  218.0 7.2 %collective-permute-start.11 = (f32[32,1,128]{2,1,0:T(1,128)S(1)}, f32[32,1,128]{2,1,0:T(1,128)S(1)}, u32[]{:S(2)}, u32[]{:S(2)}) collective-permute-start(f32[32,1,128]{2,1,0:T(1,128)S(1)} %get-tuple-element.32), channel_id=1, source_target_pairs={{0,16},{16,32},{32,48},{48,64},{64,80},{80,96},{96,112},{112,128},... | collective-permute-start | bytes 49160 | tf_op jit(solution)/shard_map/ppermute | solution.py:28
  235.2 4.3 %copy-start.7 = (s32[2,32,1]{1,2,0:T(1,128)S(1)}, s32[2,32,1]{1,2,0:T(1,128)}, u32[]{:S(2)}) copy-start(s32[2,32,1]{1,2,0:T(1,128)} %param.15) | copy-start | bytes 772
  235.2 15.4 %all-to-all-start.6 = ((f32[16,32,128]{2,1,0:T(8,128)}), f32[16,32,128]{2,1,0:T(8,128)S(1)}, u32[]{:S(2)}, u32[]{:S(2)}) async-start(f32[16,32,128]{2,1,0:T(8,128)} %constant_dynamic-update-slice_fusion.48), calls=%async_computation.6 | async-start | bytes 524288 | tf_op jit(solution)/shard_map/all_to_all | solution.py:112
  257.3 3.7 %copy-start.6 = (s32[2,32,1]{1,2,0:T(1,128)S(1)}, s32[2,32,1]{1,2,0:T(1,128)}, u32[]{:S(2)}) copy-start(s32[2,32,1]{1,2,0:T(1,128)} %param.16) | copy-start | bytes 772
  257.3 15.8 %all-to-all-start.7 = ((f32[16,32,128]{2,1,0:T(8,128)}), f32[16,32,128]{2,1,0:T(8,128)S(1)}, u32[]{:S(2)}, u32[]{:S(2)}) async-start(f32[16,32,128]{2,1,0:T(8,128)} %fusion.21), calls=%async_computation.7 | async-start | bytes 524288 | tf_op jit(solution)/shard_map/all_to_all | solution.py:119
  261.1 23.3 %collective-permute-start.12 = (f32[32,1,128]{2,0,1:T(8,128)S(1)}, f32[32,1,128]{2,0,1:T(8,128)S(1)}, u32[]{:S(2)}, u32[]{:S(2)}) collective-permute-start(f32[32,1,128]{2,0,1:T(8,128)S(1)} %get-tuple-element.30), channel_id=1, source_target_pairs={{16,0},{32,16},{48,32},{64,48},{80,64},{96,80},{112,96},{128,112},... | collective-permute-start | bytes 49160 | tf_op jit(solution)/shard_map/ppermute | solution.py:31
  263.0 20.2 %copy-start.1 = (f32[32,16,128]{2,1,0:T(8,128)S(1)}, f32[32,16,128]{2,1,0:T(8,128)}, u32[]{:S(2)}) copy-start(f32[32,16,128]{2,1,0:T(8,128)} %param.13) | copy-start | bytes 786436
  263.0 21.4 %collective-permute-start.13 = (f32[32,1,128]{2,0,1:T(8,128)S(1)}, f32[32,1,128]{2,0,1:T(8,128)S(1)}, u32[]{:S(2)}, u32[]{:S(2)}) collective-permute-start(f32[32,1,128]{2,0,1:T(8,128)S(1)} %get-tuple-element.29), channel_id=1, source_target_pairs={{0,16},{16,32},{32,48},{48,64},{64,80},{80,96},{96,112},{112,128},... | collective-permute-start | bytes 49160 | tf_op jit(solution)/shard_map/ppermute | solution.py:28
  273.2 11.2 %collective-permute-start.16 = (f32[32,1,128]{2,0,1:T(8,128)S(1)}, f32[32,1,128]{2,0,1:T(8,128)S(1)}, u32[]{:S(2)}, u32[]{:S(2)}) collective-permute-start(f32[32,1,128]{2,0,1:T(8,128)S(1)} %get-tuple-element.26), channel_id=1, source_target_pairs={{16,0},{32,16},{48,32},{64,48},{80,64},{96,80},{112,96},{128,112},... | collective-permute-start | bytes 49160 | tf_op jit(solution)/shard_map/ppermute | solution.py:31
  275.1 9.3 %collective-permute-start.17 = (f32[32,1,128]{2,0,1:T(8,128)S(1)}, f32[32,1,128]{2,0,1:T(8,128)S(1)}, u32[]{:S(2)}, u32[]{:S(2)}) collective-permute-start(f32[32,1,128]{2,0,1:T(8,128)S(1)} %get-tuple-element.25), channel_id=1, source_target_pairs={{0,16},{16,32},{32,48},{48,64},{64,80},{80,96},{96,112},{112,128},... | collective-permute-start | bytes 49160 | tf_op jit(solution)/shard_map/ppermute | solution.py:28
  285.7 16.9 %collective-permute-start.18 = (f32[32,16,128]{2,0,1:T(8,128)S(1)}, f32[32,16,128]{2,0,1:T(8,128)S(1)}, u32[]{:S(2)}, u32[]{:S(2)}) collective-permute-start(f32[32,16,128]{2,0,1:T(8,128)S(1)} %fusion.70), channel_id=1, source_target_pairs={{0,16},{16,32},{32,48},{48,64},{64,80},{80,96},{96,112},{112,128},... | collective-permute-start | bytes 786440 | tf_op jit(solution)/shard_map/ppermute | solution.py:39
  292.0 10.6 %collective-permute-start.19 = (f32[32,16,128]{2,0,1:T(8,128)S(1)}, f32[32,16,128]{2,0,1:T(8,128)S(1)}, u32[]{:S(2)}, u32[]{:S(2)}) collective-permute-start(f32[32,16,128]{2,0,1:T(8,128)S(1)} %fusion.68), channel_id=1, source_target_pairs={{16,0},{32,16},{48,32},{64,48},{80,64},{96,80},{112,96},{128,112},... | collective-permute-start | bytes 786440 | tf_op jit(solution)/shard_map/ppermute | solution.py:39
  294.3 11.5 %collective-permute-start.14 = (f32[32,16,128]{2,0,1:T(8,128)S(1)}, f32[32,16,128]{2,0,1:T(8,128)S(1)}, u32[]{:S(2)}, u32[]{:S(2)}) collective-permute-start(f32[32,16,128]{2,0,1:T(8,128)S(1)} %fusion.75), channel_id=1, source_target_pairs={{0,16},{16,32},{32,48},{48,64},{64,80},{80,96},{96,112},{112,128},... | collective-permute-start | bytes 786440 | tf_op jit(solution)/shard_map/ppermute | solution.py:39
  300.4 9.9 %collective-permute-start.15 = (f32[32,16,128]{2,0,1:T(8,128)S(1)}, f32[32,16,128]{2,0,1:T(8,128)}, u32[]{:S(2)}, u32[]{:S(2)}) collective-permute-start(f32[32,16,128]{2,0,1:T(8,128)S(1)} %fusion.73), channel_id=1, source_target_pairs={{16,0},{32,16},{48,32},{64,48},{80,64},{96,80},{112,96},{128,112},... | collective-permute-start | bytes 786440 | tf_op jit(solution)/shard_map/ppermute | solution.py:39
  314.1 1.0 copy-start.2
  314.1 1.0 copy-start.3
  314.2 1.1 copy-start.4
